TPU v7x, 256 devices: a whole 4x4x8 slice. The times are simulated.
256 devices in a mesh: member: 8 (over x, y_hi), space: 32 (over y_lo, z, core).
Axes of the slice: x: 4, y: 4 (y_hi: 2, y_lo: 2; y = y_hi * 2 + y_lo), z: 8, core: 2. Of those that a mesh axis runs over, the one named last changes fastest.
Arguments:
- ensemble: bfloat16 [256, 48, 16384], P('member', None, 'space')
- inflation: float32 [256, 128], P('member'), may hold values from 0.5 to 2
- weights: bfloat16 [128, 256, 256], P('space')
- region_ids: int32 [16384], P('space'), may hold values from 0 to 127, as said below
- extinction: float32 [48], replicated, may hold values from 0.1 to 2
- obs_cols: int32 [4096], P('space'), may hold values from 0 to 16383, as said below
Outputs:
- analysis: bfloat16 [256, 48, 16384], P('member', None, 'space')
- obs_analysis: float32 [256, 4096], P('member', 'space')
Inputs may be any that keep to these rules, and one draw needn't show every extreme that they name: `region_ids`: region r belongs to index r // 4 of space. Each block of 512 columns held by one index of space holds exactly 16 columns of the regions of every index of space. `obs_cols`: each observation's column lies in the block of 512 columns held by the same index of space as the observation.
All inputs are finite; a program needn't handle non-finite values.
Results may differ from a plain program's by a relative error of at most 0.0047.
Values may be sent and summed in bfloat16 or wider, within the bound.
No kernel may reach another device: no remote copies, remote signals or barrier semaphores. Data moves between devices by JAX's collectives and lax.ppermute only.
A program may use at most 64 MiB of HBM per device.

v0:
```python
import jax
import jax.numpy as jnp
from jax import lax
from jax.sharding import PartitionSpec as P


def local(ensemble, inflation, weights, region_ids, extinction, obs_cols):
    n_space = lax.axis_size("space")
    n_member = lax.axis_size("member")
    local_members = ensemble.shape[0]
    tracers = ensemble.shape[1]
    columns = ensemble.shape[2]
    members = local_members * n_member
    reg_count = weights.shape[0]
    all_regions = inflation.shape[1]
    send_cols = columns // n_space
    slot_cols = send_cols // n_member
    own_cols = n_space * slot_cols
    owner = region_ids // reg_count
    owner_hot = (owner[:, None] == jnp.arange(n_space, dtype=jnp.int32)[None, :]).astype(jnp.int32)
    before = jnp.cumsum(owner_hot, axis=0) - owner_hot
    rank_in = jnp.sum(before * owner_hot, axis=1)
    position = owner * send_cols + rank_in
    ordering = (
        jnp.zeros((columns,), jnp.int32).at[position].set(jnp.arange(columns, dtype=jnp.int32))
    )
    labels_all = jnp.take(region_ids % reg_count, ordering).reshape(n_space, n_member, slot_cols)
    my_labels = lax.dynamic_index_in_dim(labels_all, lax.axis_index("member"), 1, keepdims=False)
    got_labels = lax.all_to_all(
        my_labels, "space", split_axis=0, concat_axis=0, tiled=True
    ).reshape(own_cols)
    summed = lax.psum(jnp.sum(ensemble, axis=0, dtype=jnp.float32), "member")
    mean = summed / members
    region_hot = (jnp.arange(all_regions, dtype=jnp.int32)[:, None] == region_ids[None, :]).astype(
        jnp.float32
    )
    factor = jnp.dot(inflation, region_hot, precision=lax.Precision.HIGHEST)
    outgoing = ((ensemble.astype(jnp.float32) - mean[None]) * factor[:, None, :]).astype(
        jnp.bfloat16
    )
    rows_major = jnp.transpose(outgoing, (2, 0, 1)).reshape(columns, local_members * tracers)
    payload = jnp.take(rows_major, ordering, axis=0).reshape(
        n_space, n_member, slot_cols, local_members * tracers
    )
    received = lax.all_to_all(
        lax.all_to_all(payload, "member", split_axis=1, concat_axis=3, tiled=True),
        "space",
        split_axis=0,
        concat_axis=0,
        tiled=True,
    )
    gathered = received.reshape(own_cols, members, tracers)
    accum = jnp.zeros((own_cols, members, tracers), jnp.float32)
    for region in range(reg_count):
        partial_prod = jnp.einsum(
            "jk,cjt->ckt", weights[region], gathered, preferred_element_type=jnp.float32
        )
        accum = accum + jnp.where((got_labels == region)[:, None, None], partial_prod, 0.0)
    increment = accum.astype(jnp.bfloat16)
    result_rows = increment
    result_rows = result_rows.reshape(n_space, 1, slot_cols, members * tracers)
    halfway = lax.all_to_all(result_rows, "space", split_axis=0, concat_axis=0, tiled=True)
    returned = lax.all_to_all(halfway, "member", split_axis=3, concat_axis=1, tiled=True)
    restored = jnp.take(returned.reshape(columns, local_members * tracers), position, axis=0)
    restored = jnp.transpose(restored.reshape(columns, local_members, tracers), (1, 2, 0))
    analysis = (mean[None] + restored.astype(jnp.float32)).astype(jnp.bfloat16)
    local_index = obs_cols - lax.axis_index("space") * columns
    picked = jnp.take(analysis, local_index, axis=2).astype(jnp.float32)
    obs_analysis = jnp.einsum("t,kto->ko", extinction, picked, precision=lax.Precision.HIGHEST)
    return (analysis, obs_analysis)


def solution(mesh):
    in_specs = (
        P("member", None, "space"),
        P("member", None),
        P("space", None, None),
        P("space"),
        P(),
        P("space"),
    )
    out_specs = (P("member", None, "space"), P("member", "space"))
    return jax.shard_map(local, mesh=mesh, in_specs=in_specs, out_specs=out_specs, check_vma=False)
```

profile of v0, /device:TPU:64, one launch (start us, length us, event | category | flops | bytes accessed | tf_op | source)
XLA Modules:
  0.0 389.3 jit_solution(15727001249137828852)
XLA Ops:
  7.2 7.2 %copy.60 = bf16[32,48,512]{1,0,2:T(8,128)(2,1)} copy(bf16[32,48,512]{2,1,0:T(8,128)(2,1)} %param.8) | data formatting | bytes 3145728 | tf_op args[0]
  14.5 4.8 %convert_reduce_fusion = f32[48,512]{0,1:T(8,128)} fusion(bf16[32,48,512]{1,0,2:T(8,128)(2,1)} %copy.60), kind=kLoop, calls=%fused_computation.6 | loop fusion | flops 1548288 | bytes 1671168 | tf_op jit(solution)/shard_map/reduce_sum | solution.py:32
  19.3 1.2 reduce-window.6
  20.5 0.2 slice_reduce_fusion
  20.9 2.4 scatter_custom_fusion
  23.3 0.2 convolution_bitcast_fusion
  23.6 3.5 gather_fusion
  27.2 83.8 %all-reduce.2.cloned.1.call-done = f32[48,512]{0,1:T(8,128)} async-done(((f32[48,512]{0,1:T(8,128)}), f32[48,512]{0,1:T(8,128)}) %all-reduce.2.cloned.1.call-update) | async-done | bytes 98320 | tf_op jit(solution)/shard_map/psum | solution.py:32
  111.0 1.0 broadcast_multiply_fusion
  112.0 5.8 %fusion.3 = bf16[512,32,48]{2,1,0:T(8,128)(2,1)} fusion(bf16[32,48,512]{1,0,2:T(8,128)(2,1)} %copy.60, f32[32,512]{0,1:T(8,128)S(1)} %copy.62, f32[48,512]{0,1:T(8,128)S(1)} %broadcast_multiply_fusion), kind=kLoop, calls=%fused_computation.11 | loop fusion | flops 3145728 | bytes 3309568 | tf_op jit(solution)/shard_map/transpose | solution.py:41
  117.8 4.4 %copy.63 = bf16[512,32,48]{0,2,1:T(8,128)(2,1)S(1)} copy(bf16[512,32,48]{2,1,0:T(8,128)(2,1)} %fusion.3) | data formatting | bytes 3145728 | tf_op jit(solution)/shard_map/transpose | solution.py:41
  122.3 0.7 copy.64
  123.0 2.9 gather_fusion.2
  125.9 1.6 broadcast_select_fusion
  127.6 0.6 reshape.100
  128.2 2.4 copy.65
  130.6 3.6 all-to-all-start.1
  134.3 0.6 constant_dynamic-slice_fusion
  134.9 16.7 %all-to-all-done.1 = bf16[32,8,2,1536]{3,2,0,1:T(2,128)(2,1)S(1)} async-done(((bf16[32,8,2,1536]{3,2,0,1:T(2,128)(2,1)}), bf16[32,8,2,1536]{3,2,0,1:T(2,128)(2,1)S(1)}, u32[]{:S(2)}, u32[]{:S(2)}) %all-to-all-start.1) | async-done | bytes 1572896 | tf_op jit(solution)/shard_map/all_to_all | solution.py:46
  151.6 8.0 %all-to-all-start = ((s32[32,1,2]{2,1,0:T(1,128)}), s32[32,1,2]{2,1,0:T(1,128)S(1)}, u32[]{:S(2)}, u32[]{:S(2)}) async-start(s32[32,1,2]{2,1,0:T(1,128)} %constant_dynamic-slice_fusion), calls=%async_computation | async-start | bytes 32768 | tf_op jit(solution)/shard_map/all_to_all | solution.py:29
  159.6 1.3 copy.85
  160.9 2.1 reshape.160
  163.0 2.8 all-to-all-done
  165.8 6.0 %all-to-all-start.2 = ((bf16[32,1,2,12288]{3,2,1,0:T(2,128)(2,1)}), bf16[32,1,2,12288]{3,2,1,0:T(2,128)(2,1)S(1)}, u32[]{:S(2)}, u32[]{:S(2)}) async-start(bf16[32,1,2,12288]{3,2,1,0:T(2,128)(2,1)} %reshape.160), calls=%async_computation.2 | async-start | bytes 3145728 | tf_op jit(solution)/shard_map/all_to_all | solution.py:45
  172.5 37.2 %all-to-all-done.2 = bf16[32,1,2,12288]{3,2,1,0:T(2,128)(2,1)S(1)} async-done(((bf16[32,1,2,12288]{3,2,1,0:T(2,128)(2,1)}), bf16[32,1,2,12288]{3,2,1,0:T(2,128)(2,1)S(1)}, u32[]{:S(2)}, u32[]{:S(2)}) %all-to-all-start.2) | async-done | bytes 1572896 | tf_op jit(solution)/shard_map/all_to_all | solution.py:45
  209.6 5.2 %reshape.101 = bf16[64,256,48]{2,1,0:T(8,128)(2,1)} reshape(bf16[32,1,2,12288]{3,2,1,0:T(2,128)(2,1)S(1)} %all-to-all-done.2) | data formatting | bytes 3145728 | tf_op jit(solution)/shard_map/reshape | solution.py:52
  214.8 3.6 fusion.10
  218.4 1.3 fusion.12
  219.7 1.3 fusion.8
  221.0 2.3 fusion.4
  223.3 3.2 copy.72
  226.4 9.3 %reshape.102 = bf16[32,1,2,12288]{3,2,0,1:T(2,128)(2,1)S(1)} reshape(bf16[64,256,48]{2,1,0:T(8,128)(2,1)} %copy.72) | data formatting | bytes 3145728 | tf_op jit(solution)/shard_map/reshape | solution.py:61
  235.7 44.2 %all_to_all.49 = bf16[32,1,2,12288]{3,2,1,0:T(2,128)(2,1)S(1)} all-to-all(bf16[32,1,2,12288]{3,2,1,0:T(2,128)(2,1)S(1)} %bitcast.79), channel_id=1, replica_groups=mesh['member'=8,'space'=32] {'space'}, dimensions={0} | all-to-all | bytes 3145728 | tf_op jit(solution)/shard_map/all_to_all | solution.py:62
  280.0 11.1 %copy.74 = bf16[32,1,2,12288]{0,2,1,3:T(2,128)(2,1)} copy(bf16[32,1,2,12288]{3,2,1,0:T(2,128)(2,1)S(1)} %all_to_all.49) | data formatting | bytes 3145728 | tf_op jit(solution)/shard_map/all_to_all | solution.py:62
  291.1 9.5 %reshape.168 = bf16[8,2,49152]{2,1,0:T(2,128)(2,1)} reshape(bf16[12288,1,2,32]{3,2,1,0:T(2,128)(2,1)} %bitcast.74) | data formatting | bytes 3145728
  300.6 4.8 %all-to-all-start.4 = ((bf16[8,2,49152]{2,1,0:T(2,128)(2,1)}), bf16[8,2,49152]{2,1,0:T(2,128)(2,1)S(1)}, u32[]{:S(2)}, u32[]{:S(2)}) async-start(bf16[8,2,49152]{2,1,0:T(2,128)(2,1)} %reshape.168), calls=%async_computation.4 | async-start | bytes 3145728 | tf_op jit(solution)/shard_map/all_to_all | solution.py:63
  305.4 24.0 %all-to-all-done.4 = bf16[8,2,49152]{2,1,0:T(2,128)(2,1)S(1)} async-done(((bf16[8,2,49152]{2,1,0:T(2,128)(2,1)}), bf16[8,2,49152]{2,1,0:T(2,128)(2,1)S(1)}, u32[]{:S(2)}, u32[]{:S(2)}) %all-to-all-start.4) | async-done | bytes 1572896 | tf_op jit(solution)/shard_map/all_to_all | solution.py:63
  329.4 5.4 %reshape.169 = bf16[12288,1,2,32]{3,2,1,0:T(2,128)(2,1)} reshape(bf16[8,2,49152]{2,1,0:T(2,128)(2,1)S(1)} %all-to-all-done.4) | data formatting | bytes 3145728
  334.9 14.4 %copy.75 = bf16[32,1,2,8,1536]{4,2,3,0,1:T(2,128)(2,1)S(1)} copy(bf16[32,1,2,8,1536]{0,2,4,3,1:T(2,128)(2,1)} %bitcast.75) | data formatting | bytes 3145728 | tf_op jit(solution)/shard_map/all_to_all | solution.py:63
  349.3 0.6 reshape.103
  349.9 2.9 gather_fusion.3
  352.9 1.7 select_convert_fusion
  354.6 2.5 copy.76
  357.0 8.8 %copy.77 = f32[512,32,48]{2,1,0:T(8,128)} copy(f32[512,32,48]{0,2,1:T(8,128)} %bitcast.76) | data formatting | bytes 6291456 | tf_op jit(solution)/shard_map/convert_element_type | solution.py:66
  365.8 6.5 %fusion.2 = bf16[32,48,512]{1,0,2:T(8,128)(2,1)} fusion(f32[512,32,48]{2,1,0:T(8,128)} %copy.77, f32[48,512]{0,1:T(8,128)S(1)} %broadcast_multiply_fusion), kind=kLoop, calls=%fused_computation.10 | loop fusion | flops 1572864 | bytes 4816896 | tf_op jit(solution)/shard_map/convert_element_type | solution.py:66
  372.3 5.4 %copy.78 = bf16[32,48,512]{2,1,0:T(8,128)(2,1)} copy(bf16[32,48,512]{1,0,2:T(8,128)(2,1)} %fusion.2) | data formatting | bytes 3145728
  377.7 2.9 gather_fusion.1
  380.8 1.6 fusion.5
  (37 shorter events, 1.4 us)
Async XLA Ops:
  7.2 16.2 %copy-start = (f32[32,128]{1,0:T(8,128)S(1)}, f32[32,128]{1,0:T(8,128)}, u32[]{:S(2)}) copy-start(f32[32,128]{1,0:T(8,128)} %param.9) | copy-start | bytes 49156
  7.2 103.9 %all-reduce.2.cloned.1.call-start = ((), (), s32[]{:S(2)}) async-start(), calls=%async_computation.5 | async-start | bytes 524288 | tf_op jit(solution)/shard_map/psum | solution.py:32
  14.5 4.8 %copy-start.4 = (s32[512]{0:T(512)S(1)}, s32[512]{0:T(512)}, u32[]{:S(2)}) copy-start(s32[512]{0:T(512)} %param.11) | copy-start | bytes 6148
  130.6 21.1 %all-to-all-start.1 = ((bf16[32,8,2,1536]{3,2,0,1:T(2,128)(2,1)}), bf16[32,8,2,1536]{3,2,0,1:T(2,128)(2,1)S(1)}, u32[]{:S(2)}, u32[]{:S(2)}) async-start(bf16[32,8,2,1536]{3,2,0,1:T(2,128)(2,1)} %copy.65), calls=%async_computation.1 | async-start | bytes 3145728 | tf_op jit(solution)/shard_map/all_to_all | solution.py:46
  151.6 14.2 %all-to-all-start = ((s32[32,1,2]{2,1,0:T(1,128)}), s32[32,1,2]{2,1,0:T(1,128)S(1)}, u32[]{:S(2)}, u32[]{:S(2)}) async-start(s32[32,1,2]{2,1,0:T(1,128)} %constant_dynamic-slice_fusion), calls=%async_computation | async-start | bytes 32768 | tf_op jit(solution)/shard_map/all_to_all | solution.py:29
  165.8 43.8 %all-to-all-start.2 = ((bf16[32,1,2,12288]{3,2,1,0:T(2,128)(2,1)}), bf16[32,1,2,12288]{3,2,1,0:T(2,128)(2,1)S(1)}, u32[]{:S(2)}, u32[]{:S(2)}) async-start(bf16[32,1,2,12288]{3,2,1,0:T(2,128)(2,1)} %reshape.160), calls=%async_computation.2 | async-start | bytes 3145728 | tf_op jit(solution)/shard_map/all_to_all | solution.py:45
  171.8 43.0 %copy-start.3 = (bf16[4,256,256]{2,1,0:T(8,128)(2,1)S(1)}, bf16[4,256,256]{2,1,0:T(8,128)(2,1)}, u32[]{:S(2)}) copy-start(bf16[4,256,256]{2,1,0:T(8,128)(2,1)} %param.10) | copy-start | bytes 1572868
  214.8 3.6 copy-start.2
  300.6 4.8 %copy-start.6 = (s32[128]{0:T(128)S(1)}, s32[128]{0:T(128)}, u32[]{:S(2)}) copy-start(s32[128]{0:T(128)} %param.13) | copy-start | bytes 1540
  300.6 28.8 %all-to-all-start.4 = ((bf16[8,2,49152]{2,1,0:T(2,128)(2,1)}), bf16[8,2,49152]{2,1,0:T(2,128)(2,1)S(1)}, u32[]{:S(2)}, u32[]{:S(2)}) async-start(bf16[8,2,49152]{2,1,0:T(2,128)(2,1)} %reshape.168), calls=%async_computation.4 | async-start | bytes 3145728 | tf_op jit(solution)/shard_map/all_to_all | solution.py:63
  372.3 8.5 %copy-start.5 = (f32[48]{0:T(128)S(1)}, f32[48]{0:T(128)}, u32[]{:S(2)}) copy-start(f32[48]{0:T(128)} %param.12) | copy-start | bytes 580
  372.3 10.1 %copy-start.1 = (f32[32,128]{1,0:T(8,128)S(1)}, f32[32,128]{1,0:T(8,128)}, u32[]{:S(2)}) copy-start(f32[32,128]{1,0:T(8,128)} %param.9) | copy-start | bytes 49156
Sparse Core Ops, SparseCore 0:
  19.4 91.6 all-reduce.1
where the time goes:
time: 391 us; the launch traced here: 389 us
  waiting for transfers between devices  165 us (42%)
  local copies, waits for them, and re-layouts  110 us (28%)
  blocking collectives  44.2 us (11%)
  other arithmetic  23.1 us (6%)
  starting transfers between devices  22.4 us (6%)
  between operations  14.4 us (4%)
  matrix products  10.2 us (3%)
    psum x1, waiting for transfers between devices, local(): summed = lax.psum(jnp.sum(ensemble, axis=0, dtype=jnp.float32), 'member')  83.8 us
    all_to_all x1, blocking collectives, local(): lax.all_to_all(result_rows, 'space', split_axis=0, concat_axis=0, tiled=T...  44.2 us
    all_to_all x1, waiting for transfers between devices, local(): lax.all_to_all(lax.all_to_all(payload, 'member', split_axis=1, concat_axi...  37.2 us
    unnamed x18, local copies, waits for them, and re-layouts  27.6 us
    all_to_all x1, waiting for transfers between devices, local(): lax.all_to_all(halfway, 'member', split_axis=3, concat_axis=1, tiled=True)  24 us
    all_to_all x1, waiting for transfers between devices, local(): lax.all_to_all(payload, 'member', split_axis=1, concat_axis=3, tiled=True)  16.7 us
    all_to_all x1, local copies, waits for them, and re-layouts, local(): lax.all_to_all(halfway, 'member', split_axis=3, concat_axis=1, tiled=True)  14.4 us
    convert_element_type x2, local copies, waits for them, and re-layouts, local(): analysis = (mean[None] + restored.astype(jnp.float32)).astype(jnp.bfloat16)  11.2 us
  transfers between devices with their start and end apart: 5, of which 5 were waited for; matrix products, arithmetic and copies ran while one was open for 3% of the time, Pallas kernels for 0%

commit v1 on v0

--- a/solution.py
+++ b/solution.py
@@ -60,7 +60,12 @@
     result_rows = increment
     result_rows = result_rows.reshape(n_space, 1, slot_cols, members * tracers)
     halfway = lax.all_to_all(result_rows, "space", split_axis=0, concat_axis=0, tiled=True)
-    returned = lax.all_to_all(halfway, "member", split_axis=3, concat_axis=1, tiled=True)
+    returned = jnp.concatenate(
+        lax.all_to_all(
+            jnp.stack(jnp.split(halfway, lax.axis_size("member"), axis=3)), "member", 0, 0
+        ),
+        axis=1,
+    )
     restored = jnp.take(returned.reshape(columns, local_members * tracers), position, axis=0)
     restored = jnp.transpose(restored.reshape(columns, local_members, tracers), (1, 2, 0))
     analysis = (mean[None] + restored.astype(jnp.float32)).astype(jnp.bfloat16)

time: 391 us -> 358 us (0.916)
  local copies, waits for them, and re-layouts: 110 us -> 78.1 us
    all_to_all x2 -> x0, local copies, waits for them, and re-layouts: 25.5 us -> none  [the longest x1 14.4 us: local(): lax.all_to_all(halfway, 'member', split_axis=3, concat_axis=1, tiled=True)]
    unnamed x18 -> x23, local copies, waits for them, and re-layouts: 27.6 us -> 18.3 us
  transfers between devices with their start and end apart: 5 -> 5, of which waited for: 5 -> 5; matrix products, arithmetic and copies ran while one was open for 3% -> 4% of each run, Pallas kernels for 0% -> 0%
where the time goes in v1:
time: 358 us; the launch traced here: 357 us
  waiting for transfers between devices  165 us (46%)
  local copies, waits for them, and re-layouts  78.1 us (22%)
  blocking collectives  44.2 us (12%)
  other arithmetic  23.1 us (6%)
  starting transfers between devices  22.4 us (6%)
  between operations  14.4 us (4%)
  matrix products  10.2 us (3%)
    psum x1, waiting for transfers between devices, local(): summed = lax.psum(jnp.sum(ensemble, axis=0, dtype=jnp.float32), 'member')  83.8 us
    all_to_all x1, blocking collectives, local(): lax.all_to_all(result_rows, 'space', split_axis=0, concat_axis=0, tiled=T...  44.2 us
    all_to_all x1, waiting for transfers between devices, local(): lax.all_to_all(lax.all_to_all(payload, 'member', split_axis=1, concat_axi...  37.2 us
    all_to_all x1, waiting for transfers between devices, local(): lax.all_to_all(jnp.stack(jnp.split(halfway, lax.axis_size('member'), axis...  24 us
    unnamed x23, local copies, waits for them, and re-layouts  18.3 us
    all_to_all x1, waiting for transfers between devices, local(): lax.all_to_all(payload, 'member', split_axis=1, concat_axis=3, tiled=True)  16.7 us
    convert_element_type x2, local copies, waits for them, and re-layouts, local(): analysis = (mean[None] + restored.astype(jnp.float32)).astype(jnp.bfloat16)  11.2 us
    reshape x1, local copies, waits for them, and re-layouts, local(): result_rows = result_rows.reshape(n_space, 1, slot_cols, members * tracers)  9.29 us
  transfers between devices with their start and end apart: 5, of which 5 were waited for; matrix products, arithmetic and copies ran while one was open for 4% of the time, Pallas kernels for 0%

profile of v1, /device:TPU:64, one launch (start us, length us, event | category | flops | bytes accessed | tf_op | source)
XLA Modules:
  0.0 357.0 jit_solution(11227313663717926934)
XLA Ops:
  7.2 7.2 %copy.54 = bf16[32,48,512]{1,0,2:T(8,128)(2,1)} copy(bf16[32,48,512]{2,1,0:T(8,128)(2,1)} %param.8) | data formatting | bytes 3145728 | tf_op args[0]
  14.5 4.8 %convert_reduce_fusion = f32[48,512]{0,1:T(8,128)} fusion(bf16[32,48,512]{1,0,2:T(8,128)(2,1)} %copy.54), kind=kLoop, calls=%fused_computation.6 | loop fusion | flops 1548288 | bytes 1671168 | tf_op jit(solution)/shard_map/reduce_sum | solution.py:32
  19.3 1.2 reduce-window.6
  20.9 2.4 scatter_custom_fusion
  23.6 3.5 gather_fusion
  27.2 83.8 %all-reduce.2.cloned.1.call-done = f32[48,512]{0,1:T(8,128)} async-done(((f32[48,512]{0,1:T(8,128)}), f32[48,512]{0,1:T(8,128)}) %all-reduce.2.cloned.1.call-update) | async-done | bytes 98320 | tf_op jit(solution)/shard_map/psum | solution.py:32
  111.0 1.0 broadcast_multiply_fusion
  112.0 5.8 %fusion.3 = bf16[512,32,48]{2,1,0:T(8,128)(2,1)} fusion(bf16[32,48,512]{1,0,2:T(8,128)(2,1)} %copy.54, f32[32,512]{0,1:T(8,128)S(1)} %copy.56, f32[48,512]{0,1:T(8,128)S(1)} %broadcast_multiply_fusion), kind=kLoop, calls=%fused_computation.11 | loop fusion | flops 3145728 | bytes 3309568 | tf_op jit(solution)/shard_map/transpose | solution.py:41
  117.8 4.4 %copy.57 = bf16[512,32,48]{0,2,1:T(8,128)(2,1)S(1)} copy(bf16[512,32,48]{2,1,0:T(8,128)(2,1)} %fusion.3) | data formatting | bytes 3145728 | tf_op jit(solution)/shard_map/transpose | solution.py:41
  122.3 0.7 copy.58
  123.0 2.9 gather_fusion.2
  125.9 1.6 broadcast_select_fusion
  128.2 2.4 copy.59
  130.6 3.6 %all-to-all-start.1 = ((bf16[32,8,2,1536]{3,2,0,1:T(2,128)(2,1)}), bf16[32,8,2,1536]{3,2,0,1:T(2,128)(2,1)S(1)}, u32[]{:S(2)}, u32[]{:S(2)}) async-start(bf16[32,8,2,1536]{3,2,0,1:T(2,128)(2,1)} %copy.59), calls=%async_computation.1 | async-start | bytes 3145728 | tf_op jit(solution)/shard_map/all_to_all | solution.py:46
  134.9 16.7 %all-to-all-done.1 = bf16[32,8,2,1536]{3,2,0,1:T(2,128)(2,1)S(1)} async-done(((bf16[32,8,2,1536]{3,2,0,1:T(2,128)(2,1)}), bf16[32,8,2,1536]{3,2,0,1:T(2,128)(2,1)S(1)}, u32[]{:S(2)}, u32[]{:S(2)}) %all-to-all-start.1) | async-done | bytes 1572896 | tf_op jit(solution)/shard_map/all_to_all | solution.py:46
  151.6 8.0 %all-to-all-start = ((s32[32,1,2]{2,1,0:T(1,128)}), s32[32,1,2]{2,1,0:T(1,128)S(1)}, u32[]{:S(2)}, u32[]{:S(2)}) async-start(s32[32,1,2]{2,1,0:T(1,128)} %constant_dynamic-slice_fusion), calls=%async_computation | async-start | bytes 32768 | tf_op jit(solution)/shard_map/all_to_all | solution.py:29
  159.6 1.3 copy.85
  160.9 2.1 reshape.159
  163.0 2.8 all-to-all-done
  165.8 6.0 %all-to-all-start.2 = ((bf16[32,1,2,12288]{3,2,1,0:T(2,128)(2,1)}), bf16[32,1,2,12288]{3,2,1,0:T(2,128)(2,1)S(1)}, u32[]{:S(2)}, u32[]{:S(2)}) async-start(bf16[32,1,2,12288]{3,2,1,0:T(2,128)(2,1)} %reshape.159), calls=%async_computation.2 | async-start | bytes 3145728 | tf_op jit(solution)/shard_map/all_to_all | solution.py:45
  172.5 37.2 %all-to-all-done.2 = bf16[32,1,2,12288]{3,2,1,0:T(2,128)(2,1)S(1)} async-done(((bf16[32,1,2,12288]{3,2,1,0:T(2,128)(2,1)}), bf16[32,1,2,12288]{3,2,1,0:T(2,128)(2,1)S(1)}, u32[]{:S(2)}, u32[]{:S(2)}) %all-to-all-start.2) | async-done | bytes 1572896 | tf_op jit(solution)/shard_map/all_to_all | solution.py:45
  209.6 5.2 %reshape.100 = bf16[64,256,48]{2,1,0:T(8,128)(2,1)} reshape(bf16[32,1,2,12288]{3,2,1,0:T(2,128)(2,1)S(1)} %all-to-all-done.2) | data formatting | bytes 3145728 | tf_op jit(solution)/shard_map/reshape | solution.py:52
  214.8 3.6 %fusion.16 = f32[64,48,256]{2,1,0:T(8,128)S(1)} fusion(bf16[64,256,48]{2,1,0:T(8,128)(2,1)} %reshape.100, bf16[4,256,256]{2,1,0:T(8,128)(2,1)S(1)} %copy-done.3), kind=kOutput, calls=%fused_computation.38 | convolution fusion | flops 402653184 | bytes 4849664 | tf_op jit(solution)/shard_map/jk,cjt->ckt/dot_general | solution.py:55
  218.4 1.3 fusion.18
  219.7 1.3 fusion.20
  221.0 2.3 fusion.4
  223.3 3.2 copy.66
  226.4 9.3 %reshape.101 = bf16[32,1,2,12288]{3,2,0,1:T(2,128)(2,1)S(1)} reshape(bf16[64,256,48]{2,1,0:T(8,128)(2,1)} %copy.66) | data formatting | bytes 3145728 | tf_op jit(solution)/shard_map/reshape | solution.py:61
  235.7 44.2 %all_to_all.39 = bf16[32,1,2,12288]{3,2,1,0:T(2,128)(2,1)S(1)} all-to-all(bf16[32,1,2,12288]{3,2,1,0:T(2,128)(2,1)S(1)} %bitcast.121), channel_id=1, replica_groups=mesh['member'=8,'space'=32] {'space'}, dimensions={0} | all-to-all | bytes 3145728 | tf_op jit(solution)/shard_map/all_to_all | solution.py:62
  280.0 0.8 fusion.14
  280.8 0.8 fusion.13
  281.6 0.8 fusion.12
  282.4 0.8 fusion.11
  283.2 0.8 fusion.10
  284.1 0.8 fusion.9
  284.9 0.8 fusion.8
  285.7 0.8 fusion.7
  286.5 4.8 %all-to-all-start.4 = ((bf16[8,32,1,2,1536]{4,3,1,2,0:T(2,128)(2,1)}), bf16[8,32,1,2,1536]{4,3,1,2,0:T(2,128)(2,1)S(1)}, u32[]{:S(2)}, u32[]{:S(2)}) async-start(bf16[8,32,1,2,1536]{4,3,1,2,0:T(2,128)(2,1)} %fusion.7), calls=%async_computation.4 | async-start | bytes 3145728 | tf_op jit(solution)/shard_map/all_to_all | solution.py:64
  291.4 24.0 %all-to-all-done.4 = bf16[8,32,1,2,1536]{4,3,1,2,0:T(2,128)(2,1)S(1)} async-done(((bf16[8,32,1,2,1536]{4,3,1,2,0:T(2,128)(2,1)}), bf16[8,32,1,2,1536]{4,3,1,2,0:T(2,128)(2,1)S(1)}, u32[]{:S(2)}, u32[]{:S(2)}) %all-to-all-start.4) | async-done | bytes 1572896 | tf_op jit(solution)/shard_map/all_to_all | solution.py:64
  315.3 1.6 copy.75
  317.6 2.9 gather_fusion.3
  320.6 1.7 select_convert_fusion
  322.3 2.5 copy.76
  324.7 8.8 %copy.77 = f32[512,32,48]{2,1,0:T(8,128)} copy(f32[512,32,48]{0,2,1:T(8,128)} %bitcast.110) | data formatting | bytes 6291456 | tf_op jit(solution)/shard_map/convert_element_type | solution.py:71
  333.5 6.5 %fusion.2 = bf16[32,48,512]{1,0,2:T(8,128)(2,1)} fusion(f32[512,32,48]{2,1,0:T(8,128)} %copy.77, f32[48,512]{0,1:T(8,128)S(1)} %broadcast_multiply_fusion), kind=kLoop, calls=%fused_computation.10 | loop fusion | flops 1572864 | bytes 4816896 | tf_op jit(solution)/shard_map/convert_element_type | solution.py:71
  340.0 5.3 %copy.78 = bf16[32,48,512]{2,1,0:T(8,128)(2,1)} copy(bf16[32,48,512]{1,0,2:T(8,128)(2,1)} %fusion.2) | data formatting | bytes 3145728
  345.3 3.0 gather_fusion.1
  348.5 1.6 fusion.5
  (41 shorter events, 3.8 us)
Async XLA Ops:
  7.2 16.2 %copy-start = (f32[32,128]{1,0:T(8,128)S(1)}, f32[32,128]{1,0:T(8,128)}, u32[]{:S(2)}) copy-start(f32[32,128]{1,0:T(8,128)} %param.9) | copy-start | bytes 49156
  7.2 103.9 %all-reduce.2.cloned.1.call-start = ((), (), s32[]{:S(2)}) async-start(), calls=%async_computation.5 | async-start | bytes 524288 | tf_op jit(solution)/shard_map/psum | solution.py:32
  14.5 4.8 %copy-start.4 = (s32[512]{0:T(512)S(1)}, s32[512]{0:T(512)}, u32[]{:S(2)}) copy-start(s32[512]{0:T(512)} %param.11) | copy-start | bytes 6148
  130.6 21.1 %all-to-all-start.1 = ((bf16[32,8,2,1536]{3,2,0,1:T(2,128)(2,1)}), bf16[32,8,2,1536]{3,2,0,1:T(2,128)(2,1)S(1)}, u32[]{:S(2)}, u32[]{:S(2)}) async-start(bf16[32,8,2,1536]{3,2,0,1:T(2,128)(2,1)} %copy.59), calls=%async_computation.1 | async-start | bytes 3145728 | tf_op jit(solution)/shard_map/all_to_all | solution.py:46
  151.6 14.2 %all-to-all-start = ((s32[32,1,2]{2,1,0:T(1,128)}), s32[32,1,2]{2,1,0:T(1,128)S(1)}, u32[]{:S(2)}, u32[]{:S(2)}) async-start(s32[32,1,2]{2,1,0:T(1,128)} %constant_dynamic-slice_fusion), calls=%async_computation | async-start | bytes 32768 | tf_op jit(solution)/shard_map/all_to_all | solution.py:29
  165.8 43.8 %all-to-all-start.2 = ((bf16[32,1,2,12288]{3,2,1,0:T(2,128)(2,1)}), bf16[32,1,2,12288]{3,2,1,0:T(2,128)(2,1)S(1)}, u32[]{:S(2)}, u32[]{:S(2)}) async-start(bf16[32,1,2,12288]{3,2,1,0:T(2,128)(2,1)} %reshape.159), calls=%async_computation.2 | async-start | bytes 3145728 | tf_op jit(solution)/shard_map/all_to_all | solution.py:45
  172.5 42.3 %copy-start.3 = (bf16[4,256,256]{2,1,0:T(8,128)(2,1)S(1)}, bf16[4,256,256]{2,1,0:T(8,128)(2,1)}, u32[]{:S(2)}) copy-start(bf16[4,256,256]{2,1,0:T(8,128)(2,1)} %param.10) | copy-start | bytes 1572868
  214.8 3.6 %copy-start.2 = (bf16[64,256,48]{2,1,0:T(8,128)(2,1)S(1)}, bf16[64,256,48]{2,1,0:T(8,128)(2,1)}, u32[]{:S(2)}) copy-start(bf16[64,256,48]{2,1,0:T(8,128)(2,1)} %reshape.100) | copy-start | bytes 4718596
  286.5 4.8 %copy-start.6 = (s32[128]{0:T(128)S(1)}, s32[128]{0:T(128)}, u32[]{:S(2)}) copy-start(s32[128]{0:T(128)} %param.13) | copy-start | bytes 1540
  286.5 28.8 %all-to-all-start.4 = ((bf16[8,32,1,2,1536]{4,3,1,2,0:T(2,128)(2,1)}), bf16[8,32,1,2,1536]{4,3,1,2,0:T(2,128)(2,1)S(1)}, u32[]{:S(2)}, u32[]{:S(2)}) async-start(bf16[8,32,1,2,1536]{4,3,1,2,0:T(2,128)(2,1)} %fusion.7), calls=%async_computation.4 | async-start | bytes 3145728 | tf_op jit(solution)/shard_map/all_to_all | solution.py:64
  345.3 3.2 copy-start.5
  348.3 1.8 copy-start.1
Sparse Core Ops, SparseCore 0:
  19.4 91.6 all-reduce.1
